TPU v7x, 512 devices: a whole 4x4x16 slice. The times are simulated.
512 devices in a mesh: blk: 32 (over z, core), col: 16 (over y, x).
Axes of the slice: x: 4, y: 4, z: 16, core: 2. Of those that a mesh axis runs over, the one named last changes fastest.
Arguments:
- density: float32 [96, 7, 256, 256], P('blk', None, 'col'), as said below
- band_widths: int32 [96], P('blk'), may hold values from 1 to 3, as said below
Outputs:
- purified: float32 [96, 7, 256, 256], P('blk', None, 'col')
Inputs may be any that keep to these rules, and one draw needn't show every extreme that they name: `band_widths`: each block row keeps between 1 and 3 blocks on each side; 3 is reached in every draw. `density`: diagonal entries of the diagonal blocks lie between 0.05 and 0.95, all other entries are small.
All inputs are finite; a program needn't handle non-finite values.
Results may differ from a plain program's by a relative error of at most 0.00013.
Values sent between devices are 32-bit elements; how exact they have to be, the bound alone decides.
No kernel may reach another device: no remote copies, remote signals or barrier semaphores. Data moves between devices by JAX's collectives and lax.ppermute only.
A program may use at most 64 MiB of HBM per device.

v0:
```python
import jax
import jax.numpy as jnp
from jax import lax
from jax.sharding import PartitionSpec as P

W = 3


def send(cells, shift):
    count = lax.axis_size("blk")
    return lax.ppermute(cells, "blk", [(i, (i + shift) % count) for i in range(count)])


def halo_pieces(cells):
    rows = cells.shape[0]
    tail = [cells[rows - W + k, W - k :] for k in range(W)]
    head = [cells[k, : 2 * W - k] for k in range(W)]
    return (tail, head)


def extend(right):
    tail, head = halo_pieces(right)
    from_left = send(jnp.concatenate(tail, axis=0), 1)
    from_right = send(jnp.concatenate(head, axis=0), -1)
    zero = jnp.zeros((1,) + right.shape[2:], right.dtype)
    rows = []
    start = 0
    for k in range(W):
        width = 2 * W + 1 - (W - k)
        piece = from_left[start : start + width]
        start += width
        rows.append(
            jnp.concatenate([jnp.broadcast_to(zero, (W - k,) + right.shape[2:]), piece], axis=0)
        )
    left = jnp.stack(rows)
    rows = []
    start = 0
    for k in range(W):
        width = 2 * W - k
        piece = from_right[start : start + width]
        start += width
        rows.append(
            jnp.concatenate([piece, jnp.broadcast_to(zero, (k + 1,) + right.shape[2:])], axis=0)
        )
    right_rows = jnp.stack(rows)
    return jnp.concatenate([left, right, right_rows], axis=0)


def contract(extended, shard_rows, keep=None):
    local_rows = shard_rows.shape[0]
    span = 2 * W + 1
    zeros = jnp.zeros_like(extended[:local_rows, :1])
    shifted = []
    for inner_band in range(span):
        window = extended[inner_band : inner_band + local_rows]
        shift = inner_band - W
        if shift > 0:
            window = jnp.concatenate([zeros] * shift + [window[:, : span - shift]], axis=1)
        elif shift < 0:
            window = jnp.concatenate([window[:, -shift:]] + [zeros] * -shift, axis=1)
        shifted.append(window)
    stacked = jnp.stack(shifted, axis=3)
    if keep is not None:
        shard_rows = shard_rows * keep
    return jnp.einsum("ibcas,iasr->ibcr", stacked, shard_rows, precision=lax.Precision.HIGH)


def on_device(density, band_widths):
    offsets = jnp.abs(jnp.arange(2 * W + 1, dtype=jnp.int32) - W)
    pattern = (offsets[None, :] <= band_widths[:, None]).astype(jnp.float32)[:, :, None, None]
    current = density * pattern
    for purify_step in range(2):
        if purify_step == 0:
            gathered, keep = (lax.all_gather(density, "col", axis=2, tiled=True), pattern)
        else:
            gathered, keep = (lax.all_gather(current, "col", axis=2, tiled=True), None)
        square = contract(extend(current), gathered, keep) * pattern
        third_power = contract(extend(square), gathered, keep) * pattern
        current = 3.0 * square - 2.0 * third_power
    return current


def solution(mesh):
    in_specs = (P("blk", None, "col", None), P("blk"))
    out_specs = P("blk", None, "col", None)
    return jax.shard_map(
        on_device, mesh=mesh, in_specs=in_specs, out_specs=out_specs, check_vma=False
    )
```

profile of v0, /device:TPU:97, one launch (start us, length us, event | category | flops | bytes accessed | tf_op | source)
XLA Modules:
  0.0 198.5 jit_solution(10707903417032842990)
XLA Ops:
  6.5 0.0 all-gather.3.cloned.1.call-start
  6.5 0.7 all-gather.3.cloned.1.call-update
  7.3 0.0 all-gather.5.cloned.1.call-start
  7.3 0.7 compare_convert_fusion
  8.0 1.1 broadcast_multiply_fusion
  9.2 0.0 copy-start.2
  9.2 3.4 %collective-permute-start = (f32[15,16,256]{2,1,0:T(8,128)S(1)}, f32[15,16,256]{2,1,0:T(8,128)S(1)}, u32[]{:S(2)}, u32[]{:S(2)}) collective-permute-start(f32[15,16,256]{2,1,0:T(8,128)S(1)} %pad_maximum_fusion), channel_id=1, source_target_pairs={{0,16},{16,32},{32,48},{48,64},{64,80},{80,96},{96,112},{112,128},... | collective-permute-start | bytes 737288 | tf_op jit(solution)/shard_map/ppermute | solution.py:11
  12.7 0.0 collective-permute-start.1
  12.7 3.1 %collective-permute-done = f32[15,16,256]{2,1,0:T(8,128)S(1)} collective-permute-done((f32[15,16,256]{2,1,0:T(8,128)S(1)}, f32[15,16,256]{2,1,0:T(8,128)S(1)}, u32[]{:S(2)}, u32[]{:S(2)}) %collective-permute-start) | collective-permute-done | bytes 245792 | tf_op jit(solution)/shard_map/ppermute | solution.py:11
  15.8 3.7 %collective-permute-done.1 = f32[15,16,256]{2,1,0:T(8,128)S(1)} collective-permute-done((f32[15,16,256]{2,1,0:T(8,128)S(1)}, f32[15,16,256]{2,1,0:T(8,128)S(1)}, u32[]{:S(2)}, u32[]{:S(2)}) %collective-permute-start.1) | collective-permute-done | bytes 245792 | tf_op jit(solution)/shard_map/ppermute | solution.py:11
  19.7 0.0 copy-done.2
  19.7 0.1 fusion.84
  19.8 0.0 copy-done.1
  19.8 0.1 bitcast_dynamic-update-slice_fusion
  20.0 66.8 %all-gather.3.cloned.1.call-done = f32[3,7,256,256]{3,2,1,0:T(8,128)} async-done(((f32[3,7,16,256]{3,2,1,0:T(8,128)}), f32[3,7,256,256]{3,2,1,0:T(8,128)}) %all-gather.3.cloned.1.call-update) | async-done | bytes 5505040 | tf_op jit(solution)/shard_map/all_gather | solution.py:74
  86.8 4.4 %fusion.16 = f32[3,7,16,256]{3,2,1,0:T(8,128)S(1)} fusion(f32[3,7,16,7,256]{4,2,3,1,0:T(8,128)S(1)} %fusion.68, f32[3,7,256,256]{3,2,1,0:T(8,128)} %all-gather.3.cloned.1.call-done, f32[3,7]{1,0:T(4,128)S(1)} %compare_convert_fusion), kind=kOutput, calls=%fused_computation.15 | convolution fusion | flops 926306304 | bytes 8257620 | tf_op jit(solution)/shard_map/ibcas,iasr->ibcr/dot_general | solution.py:65
  91.2 0.0 slice-start.1
  91.3 3.1 %collective-permute-start.2 = (f32[15,16,256]{2,1,0:T(8,128)S(1)}, f32[15,16,256]{2,1,0:T(8,128)S(1)}, u32[]{:S(2)}, u32[]{:S(2)}) collective-permute-start(f32[15,16,256]{2,1,0:T(8,128)S(1)} %pad_maximum_fusion.2), channel_id=1, source_target_pairs={{0,16},{16,32},{32,48},{48,64},{64,80},{80,96},{96,112},{112,128},... | collective-permute-start | bytes 737288 | tf_op jit(solution)/shard_map/ppermute | solution.py:11
  94.4 0.0 collective-permute-start.3
  94.4 3.1 %collective-permute-done.2 = f32[15,16,256]{2,1,0:T(8,128)S(1)} collective-permute-done((f32[15,16,256]{2,1,0:T(8,128)S(1)}, f32[15,16,256]{2,1,0:T(8,128)S(1)}, u32[]{:S(2)}, u32[]{:S(2)}) %collective-permute-start.2) | collective-permute-done | bytes 245792 | tf_op jit(solution)/shard_map/ppermute | solution.py:11
  97.7 3.5 %collective-permute-done.3 = f32[15,16,256]{2,1,0:T(8,128)S(1)} collective-permute-done((f32[15,16,256]{2,1,0:T(8,128)S(1)}, f32[15,16,256]{2,1,0:T(8,128)S(1)}, u32[]{:S(2)}, u32[]{:S(2)}) %collective-permute-start.3) | collective-permute-done | bytes 245792 | tf_op jit(solution)/shard_map/ppermute | solution.py:11
  101.3 0.1 fusion.83
  101.4 0.0 slice-done
  101.5 0.0 slice-done.1
  101.5 1.7 fusion.2
  103.2 0.8 fusion.80
  104.0 0.0 all-gather.5.cloned.1.call-update
  104.0 0.9 slice_bitcast_fusion.18
  105.0 1.0 slice_bitcast_fusion.10
  106.0 1.0 slice_bitcast_fusion.2
  106.9 0.2 collective-permute-start.4
  107.2 0.3 collective-permute-start.5
  107.5 2.8 %collective-permute-done.4 = f32[15,16,256]{2,1,0:T(8,128)S(1)} collective-permute-done((f32[15,16,256]{2,1,0:T(8,128)S(1)}, f32[15,16,256]{2,1,0:T(8,128)S(1)}, u32[]{:S(2)}, u32[]{:S(2)}) %collective-permute-start.4) | collective-permute-done | bytes 245792 | tf_op jit(solution)/shard_map/ppermute | solution.py:11
  110.3 3.7 %collective-permute-done.5 = f32[15,16,256]{2,1,0:T(8,128)S(1)} collective-permute-done((f32[15,16,256]{2,1,0:T(8,128)S(1)}, f32[15,16,256]{2,1,0:T(8,128)S(1)}, u32[]{:S(2)}, u32[]{:S(2)}) %collective-permute-start.5) | collective-permute-done | bytes 245792 | tf_op jit(solution)/shard_map/ppermute | solution.py:11
  114.2 0.0 copy-done
  114.2 0.1 fusion.82
  114.4 59.8 %all-gather.5.cloned.1.call-done = f32[3,7,256,256]{3,2,1,0:T(8,128)} async-done(((f32[3,7,16,256]{3,2,1,0:T(8,128)}), f32[3,7,256,256]{3,2,1,0:T(8,128)}) %all-gather.5.cloned.1.call-update) | async-done | bytes 5505040 | tf_op jit(solution)/shard_map/all_gather | solution.py:76
  174.2 4.4 %fusion.6 = f32[3,7,16,256,1]{3,2,0,1,4:T(8,128)S(1)} fusion(f32[3,7,16,7,256]{4,2,1,0,3:T(8,128)S(1)} %fusion.32, f32[3,7,256,256]{3,2,1,0:T(8,128)} %all-gather.5.cloned.1.call-done), kind=kOutput, calls=%fused_computation.6 | convolution fusion | flops 924844032 | bytes 8257536 | tf_op jit(solution)/shard_map/ibcas,iasr->ibcr/dot_general | solution.py:65
  178.7 0.1 bitcast_multiply_fusion.1
  178.8 0.0 slice-start.3
  178.9 3.1 %collective-permute-start.6 = (f32[15,16,256]{2,1,0:T(8,128)S(1)}, f32[15,16,256]{2,1,0:T(8,128)S(1)}, u32[]{:S(2)}, u32[]{:S(2)}) collective-permute-start(f32[15,16,256]{2,1,0:T(8,128)S(1)} %pad_maximum_fusion.6), channel_id=1, source_target_pairs={{0,16},{16,32},{32,48},{48,64},{64,80},{80,96},{96,112},{112,128},... | collective-permute-start | bytes 737288 | tf_op jit(solution)/shard_map/ppermute | solution.py:11
  181.9 0.0 collective-permute-start.7
  182.0 3.1 %collective-permute-done.6 = f32[15,16,256]{2,1,0:T(8,128)S(1)} collective-permute-done((f32[15,16,256]{2,1,0:T(8,128)S(1)}, f32[15,16,256]{2,1,0:T(8,128)S(1)}, u32[]{:S(2)}, u32[]{:S(2)}) %collective-permute-start.6) | collective-permute-done | bytes 245792 | tf_op jit(solution)/shard_map/ppermute | solution.py:11
  185.2 0.1 bitcast_dynamic-update-slice_fusion.1
  185.3 3.4 %collective-permute-done.7 = f32[15,16,256]{2,1,0:T(8,128)S(1)} collective-permute-done((f32[15,16,256]{2,1,0:T(8,128)S(1)}, f32[15,16,256]{2,1,0:T(8,128)S(1)}, u32[]{:S(2)}, u32[]{:S(2)}) %collective-permute-start.7) | collective-permute-done | bytes 245792 | tf_op jit(solution)/shard_map/ppermute | solution.py:11
  188.8 0.1 fusion.81
  189.0 1.8 fusion.4
  190.8 0.9 fusion.78
  (90 shorter events, 1.2 us)
Async XLA Ops:
  6.5 80.2 %all-gather.3.cloned.1.call-start = ((), (), s32[]{:S(2)}) async-start(), calls=%async_computation | async-start | bytes 5849088 | tf_op jit(solution)/shard_map/all_gather | solution.py:74
  7.3 167.0 %all-gather.5.cloned.1.call-start = ((), (), s32[]{:S(2)}) async-start(), calls=%async_computation.1 | async-start | bytes 5849088 | tf_op jit(solution)/shard_map/all_gather | solution.py:76
  9.2 10.5 %copy-start.2 = (pred[7]{0:T(512)(128)(4,1)S(1)}, pred[7]{0:T(512)(128)(4,1)}, u32[]{:S(2)}) copy-start(pred[7]{0:T(512)(128)(4,1)} %constant.7.clone.1) | copy-start | bytes 25
  9.2 6.6 %collective-permute-start = (f32[15,16,256]{2,1,0:T(8,128)S(1)}, f32[15,16,256]{2,1,0:T(8,128)S(1)}, u32[]{:S(2)}, u32[]{:S(2)}) collective-permute-start(f32[15,16,256]{2,1,0:T(8,128)S(1)} %pad_maximum_fusion), channel_id=1, source_target_pairs={{0,16},{16,32},{32,48},{48,64},{64,80},{80,96},{96,112},{112,128},... | collective-permute-start | bytes 737288 | tf_op jit(solution)/shard_map/ppermute | solution.py:11
  12.6 7.1 %copy-start.1 = (f32[3,7,16,256]{3,2,1,0:T(8,128)S(1)}, f32[3,7,16,256]{3,2,1,0:T(8,128)}, u32[]{:S(2)}) copy-start(f32[3,7,16,256]{3,2,1,0:T(8,128)} %param.2) | copy-start | bytes 1032196
  12.7 6.8 %collective-permute-start.1 = (f32[15,16,256]{2,1,0:T(8,128)S(1)}, f32[15,16,256]{2,1,0:T(8,128)S(1)}, u32[]{:S(2)}, u32[]{:S(2)}) collective-permute-start(f32[15,16,256]{2,1,0:T(8,128)S(1)} %pad_maximum_fusion.1), channel_id=1, source_target_pairs={{0,496},{16,0},{32,16},{48,32},{64,48},{80,64},{96,80},{112,96},{1... | collective-permute-start | bytes 737288 | tf_op jit(solution)/shard_map/ppermute | solution.py:11
  86.8 14.7 %slice-start = ((s8[5505024]{0:T(1024)(128)(4,1)}), s8[4194304]{0:T(1024)(128)(4,1)S(1)}, s32[]{:S(2)}) async-start(s8[5505024]{0:T(1024)(128)(4,1)} %bitcast.255), calls=%async_computation.2 | async-start | bytes 8388608
  91.2 10.2 %slice-start.1 = ((s8[5505024]{0:T(1024)(128)(4,1)}), s8[1310720]{0:T(1024)(128)(4,1)S(1)}, s32[]{:S(2)}) async-start(s8[5505024]{0:T(1024)(128)(4,1)} %bitcast.255), calls=%async_computation.3 | async-start | bytes 2621440
  91.3 6.2 %collective-permute-start.2 = (f32[15,16,256]{2,1,0:T(8,128)S(1)}, f32[15,16,256]{2,1,0:T(8,128)S(1)}, u32[]{:S(2)}, u32[]{:S(2)}) collective-permute-start(f32[15,16,256]{2,1,0:T(8,128)S(1)} %pad_maximum_fusion.2), channel_id=1, source_target_pairs={{0,16},{16,32},{32,48},{48,64},{64,80},{80,96},{96,112},{112,128},... | collective-permute-start | bytes 737288 | tf_op jit(solution)/shard_map/ppermute | solution.py:11
  94.4 6.8 %collective-permute-start.3 = (f32[15,16,256]{2,1,0:T(8,128)S(1)}, f32[15,16,256]{2,1,0:T(8,128)S(1)}, u32[]{:S(2)}, u32[]{:S(2)}) collective-permute-start(f32[15,16,256]{2,1,0:T(8,128)S(1)} %pad_maximum_fusion.3), channel_id=1, source_target_pairs={{0,496},{16,0},{32,16},{48,32},{64,48},{80,64},{96,80},{112,96},{1... | collective-permute-start | bytes 737288 | tf_op jit(solution)/shard_map/ppermute | solution.py:11
  104.0 10.1 %copy-start = (f32[3,7,16,256]{3,2,1,0:T(8,128)S(1)}, f32[3,7,16,256]{3,2,1,0:T(8,128)}, u32[]{:S(2)}) copy-start(f32[3,7,16,256]{3,2,1,0:T(8,128)} %fusion.80) | copy-start | bytes 1032196
  106.9 3.4 %collective-permute-start.4 = (f32[15,16,256]{2,1,0:T(8,128)S(1)}, f32[15,16,256]{2,1,0:T(8,128)S(1)}, u32[]{:S(2)}, u32[]{:S(2)}) collective-permute-start(f32[15,16,256]{2,1,0:T(8,128)S(1)} %pad_maximum_fusion.4), channel_id=1, source_target_pairs={{0,16},{16,32},{32,48},{48,64},{64,80},{80,96},{96,112},{112,128},... | collective-permute-start | bytes 737288 | tf_op jit(solution)/shard_map/ppermute | solution.py:11
  107.2 6.8 %collective-permute-start.5 = (f32[15,16,256]{2,1,0:T(8,128)S(1)}, f32[15,16,256]{2,1,0:T(8,128)S(1)}, u32[]{:S(2)}, u32[]{:S(2)}) collective-permute-start(f32[15,16,256]{2,1,0:T(8,128)S(1)} %pad_maximum_fusion.5), channel_id=1, source_target_pairs={{0,496},{16,0},{32,16},{48,32},{64,48},{80,64},{96,80},{112,96},{1... | collective-permute-start | bytes 737288 | tf_op jit(solution)/shard_map/ppermute | solution.py:11
  174.2 14.8 %slice-start.2 = ((s8[5505024]{0:T(1024)(128)(4,1)}), s8[4194304]{0:T(1024)(128)(4,1)S(1)}, s32[]{:S(2)}) async-start(s8[5505024]{0:T(1024)(128)(4,1)} %bitcast.257), calls=%async_computation.4 | async-start | bytes 8388608
  178.8 10.3 %slice-start.3 = ((s8[5505024]{0:T(1024)(128)(4,1)}), s8[1310720]{0:T(1024)(128)(4,1)S(1)}, s32[]{:S(2)}) async-start(s8[5505024]{0:T(1024)(128)(4,1)} %bitcast.257), calls=%async_computation.5 | async-start | bytes 2621440
  178.9 6.2 %collective-permute-start.6 = (f32[15,16,256]{2,1,0:T(8,128)S(1)}, f32[15,16,256]{2,1,0:T(8,128)S(1)}, u32[]{:S(2)}, u32[]{:S(2)}) collective-permute-start(f32[15,16,256]{2,1,0:T(8,128)S(1)} %pad_maximum_fusion.6), channel_id=1, source_target_pairs={{0,16},{16,32},{32,48},{48,64},{64,80},{80,96},{96,112},{112,128},... | collective-permute-start | bytes 737288 | tf_op jit(solution)/shard_map/ppermute | solution.py:11
  181.9 6.8 %collective-permute-start.7 = (f32[15,16,256]{2,1,0:T(8,128)S(1)}, f32[15,16,256]{2,1,0:T(8,128)S(1)}, u32[]{:S(2)}, u32[]{:S(2)}) collective-permute-start(f32[15,16,256]{2,1,0:T(8,128)S(1)} %pad_maximum_fusion.7), channel_id=1, source_target_pairs={{0,496},{16,0},{32,16},{48,32},{64,48},{80,64},{96,80},{112,96},{1... | collective-permute-start | bytes 737288 | tf_op jit(solution)/shard_map/ppermute | solution.py:11
Sparse Core Ops, SparseCore 0:
  10.4 76.3 all-gather.2
  104.2 70.0 all-gather.4
where the time goes:
time: 199 us; the launch traced here: 198 us
  waiting for transfers between devices  154 us (77%)
  between operations  14.1 us (7%)
  matrix products  12.3 us (6%)
  starting transfers between devices  10.2 us (5%)
  other arithmetic  4.81 us (2%)
  local copies, waits for them, and re-layouts  3.36 us (2%)
    all_gather x1, waiting for transfers between devices, on_device(): lax.all_gather(density, 'col', axis=2, tiled=True)  66.8 us
    all_gather x1, waiting for transfers between devices, on_device(): gathered, keep = (lax.all_gather(current, 'col', axis=2, tiled=True), None)  59.8 us
    ppermute x8, waiting for transfers between devices, send(): lax.ppermute(cells, 'blk', [(i, (i + shift) % count) for i in range(count)])  26.4 us
    dot_general x4, matrix products, contract(): jnp.einsum('ibcas,iasr->ibcr', stacked, shard_rows, precision=lax.Precisi...  12.3 us
    ppermute x8, starting transfers between devices, send(): lax.ppermute(cells, 'blk', [(i, (i + shift) % count) for i in range(count)])  10.1 us
  transfers between devices with their start and end apart: 10, of which 10 were waited for; matrix products, arithmetic and copies ran while one was open for 3% of the time, Pallas kernels for 0%

commit v1 on v0

--- a/solution.py
+++ b/solution.py
@@ -4,6 +4,11 @@
 from jax.sharding import PartitionSpec as P
 
 W = 3
+
+
+def gather_from_all(x, axis, dim):
+    copies = jnp.concatenate([x] * lax.axis_size(axis), axis=dim)
+    return lax.all_to_all(copies, axis, dim, dim, tiled=True)
 
 
 def send(cells, shift):
@@ -73,7 +78,7 @@
         if purify_step == 0:
             gathered, keep = (lax.all_gather(density, "col", axis=2, tiled=True), pattern)
         else:
-            gathered, keep = (lax.all_gather(current, "col", axis=2, tiled=True), None)
+            gathered, keep = (gather_from_all(current, "col", 2), None)
         square = contract(extend(current), gathered, keep) * pattern
         third_power = contract(extend(square), gathered, keep) * pattern
         current = 3.0 * square - 2.0 * third_power

time: 199 us -> 239 us (1.20)
  the two profiles are of different devices: /device:TPU:97 before, /device:TPU:1 now
where the time goes in v1:
time: 239 us
  waiting for transfers between devices  175 us (73%)
  starting transfers between devices  21 us (9%)
  matrix products  18 us (8%)
  between operations  14.2 us (6%)
  local copies, waits for them, and re-layouts  6.77 us (3%)
  other arithmetic  4.09 us (2%)
    all_to_all x1, waiting for transfers between devices, gather_from_all(): return lax.all_to_all(copies, axis, dim, dim, tiled=True)  85.5 us
    all_gather x1, waiting for transfers between devices, on_device(): lax.all_gather(density, 'col', axis=2, tiled=True)  70.4 us
    dot_general x4, matrix products, contract(): jnp.einsum('ibcas,iasr->ibcr', stacked, shard_rows, precision=lax.Precisi...  18 us
    ppermute x8, waiting for transfers between devices, send(): lax.ppermute(cells, 'blk', [(i, (i + shift) % count) for i in range(count)])  18 us
    ppermute x8, starting transfers between devices, send(): lax.ppermute(cells, 'blk', [(i, (i + shift) % count) for i in range(count)])  15.9 us
    concatenate x2, local copies, waits for them, and re-layouts, gather_from_all(): copies = jnp.concatenate([x] * lax.axis_size(axis), axis=dim)  5.89 us
    all_to_all x1, starting transfers between devices, gather_from_all(): return lax.all_to_all(copies, axis, dim, dim, tiled=True)  5.03 us
  transfers between devices with their start and end apart: 10, of which 10 were waited for; matrix products, arithmetic and copies ran while one was open for 1% of the time, Pallas kernels for 0%

profile of v1, /device:TPU:1, one launch (start us, length us, event | category | flops | bytes accessed | tf_op | source)
XLA Modules:
  0.0 238.7 jit_solution(17688081627496066878)
XLA Ops:
  6.5 0.0 all-gather.2.cloned.1.call-start
  6.5 0.7 all-gather.2.cloned.1.call-update
  7.3 0.7 compare_convert_fusion
  8.0 1.1 broadcast_multiply_fusion
  9.1 0.0 copy-start.1
  9.2 3.0 %collective-permute-start = (f32[15,16,256]{2,1,0:T(8,128)S(1)}, f32[15,16,256]{2,1,0:T(8,128)S(1)}, u32[]{:S(2)}, u32[]{:S(2)}) collective-permute-start(f32[15,16,256]{2,1,0:T(8,128)S(1)} %pad_maximum_fusion), channel_id=1, source_target_pairs={{0,16},{16,32},{32,48},{48,64},{64,80},{80,96},{96,112},{112,128},... | collective-permute-start | bytes 737288 | tf_op jit(solution)/shard_map/ppermute | solution.py:16
  12.2 0.0 copy-start
  12.2 3.9 %collective-permute-start.1 = (f32[15,16,256]{2,1,0:T(8,128)S(1)}, f32[15,16,256]{2,1,0:T(8,128)S(1)}, u32[]{:S(2)}, u32[]{:S(2)}) collective-permute-start(f32[15,16,256]{2,1,0:T(8,128)S(1)} %pad_maximum_fusion.1), channel_id=1, source_target_pairs={{0,496},{16,0},{32,16},{48,32},{64,48},{80,64},{96,80},{112,96},{1... | collective-permute-start | bytes 737288 | tf_op jit(solution)/shard_map/ppermute | solution.py:16
  16.1 0.9 collective-permute-done
  17.1 0.8 collective-permute-done.1
  18.0 0.0 copy-done.1
  18.0 0.1 fusion.84
  18.1 0.0 copy-done
  18.1 0.1 bitcast_dynamic-update-slice_fusion
  18.3 70.4 %all-gather.2.cloned.1.call-done = f32[3,7,256,256]{3,2,1,0:T(8,128)} async-done(((f32[3,7,16,256]{3,2,1,0:T(8,128)}), f32[3,7,256,256]{3,2,1,0:T(8,128)}) %all-gather.2.cloned.1.call-update) | async-done | bytes 5505040 | tf_op jit(solution)/shard_map/all_gather | solution.py:79
  88.7 0.0 slice-start
  88.7 4.4 %fusion.16 = f32[3,7,16,256]{3,2,1,0:T(8,128)S(1)} fusion(f32[3,7,16,7,256]{4,2,3,1,0:T(8,128)S(1)} %fusion.68, f32[3,7,256,256]{3,2,1,0:T(8,128)} %all-gather.2.cloned.1.call-done, f32[3,7]{1,0:T(4,128)S(1)} %compare_convert_fusion), kind=kOutput, calls=%fused_computation.15 | convolution fusion | flops 926306304 | bytes 8257620 | tf_op jit(solution)/shard_map/ibcas,iasr->ibcr/dot_general | solution.py:70
  93.1 0.0 slice-start.1
  93.2 1.8 collective-permute-start.2
  95.1 0.0 collective-permute-start.3
  95.1 3.1 %collective-permute-done.2 = f32[15,16,256]{2,1,0:T(8,128)S(1)} collective-permute-done((f32[15,16,256]{2,1,0:T(8,128)S(1)}, f32[15,16,256]{2,1,0:T(8,128)S(1)}, u32[]{:S(2)}, u32[]{:S(2)}) %collective-permute-start.2) | collective-permute-done | bytes 245792 | tf_op jit(solution)/shard_map/ppermute | solution.py:16
  98.4 2.5 %collective-permute-done.3 = f32[15,16,256]{2,1,0:T(8,128)S(1)} collective-permute-done((f32[15,16,256]{2,1,0:T(8,128)S(1)}, f32[15,16,256]{2,1,0:T(8,128)S(1)}, u32[]{:S(2)}, u32[]{:S(2)}) %collective-permute-start.3) | collective-permute-done | bytes 245792 | tf_op jit(solution)/shard_map/ppermute | solution.py:16
  100.9 0.1 fusion.83
  101.1 0.0 slice-done
  101.1 0.0 slice-done.1
  101.1 1.7 fusion.2
  102.8 0.1 constant_dynamic-update-slice_fusion.15
  103.5 5.9 %copy.19 = f32[3,7,256,256]{3,1,0,2:T(8,128)} copy(f32[3,7,256,256]{3,2,1,0:T(8,128)S(1)} %constant_dynamic-update-slice_fusion) | data formatting | bytes 11010048 | tf_op jit(solution)/shard_map/concatenate | solution.py:10
  109.3 5.0 %all-to-all-start = ((f32[3,7,256,256]{3,1,0,2:T(8,128)}), f32[3,7,256,256]{3,1,0,2:T(8,128)}, u32[]{:S(2)}, u32[]{:S(2)}) async-start(f32[3,7,256,256]{3,1,0,2:T(8,128)} %copy.19), calls=%async_computation | async-start | bytes 12582912 | tf_op jit(solution)/shard_map/all_to_all | solution.py:11
  114.5 0.3 collective-permute-start.4
  114.8 0.6 collective-permute-start.5
  115.5 2.5 %collective-permute-done.4 = f32[15,16,256]{2,1,0:T(8,128)S(1)} collective-permute-done((f32[15,16,256]{2,1,0:T(8,128)S(1)}, f32[15,16,256]{2,1,0:T(8,128)S(1)}, u32[]{:S(2)}, u32[]{:S(2)}) %collective-permute-start.4) | collective-permute-done | bytes 245792 | tf_op jit(solution)/shard_map/ppermute | solution.py:16
  118.0 2.9 %collective-permute-done.5 = f32[15,16,256]{2,1,0:T(8,128)S(1)} collective-permute-done((f32[15,16,256]{2,1,0:T(8,128)S(1)}, f32[15,16,256]{2,1,0:T(8,128)S(1)}, u32[]{:S(2)}, u32[]{:S(2)}) %collective-permute-start.5) | collective-permute-done | bytes 245792 | tf_op jit(solution)/shard_map/ppermute | solution.py:16
  121.1 0.1 fusion.82
  121.3 85.5 %all-to-all-done = f32[3,7,256,256]{3,1,0,2:T(8,128)} async-done(((f32[3,7,256,256]{3,1,0,2:T(8,128)}), f32[3,7,256,256]{3,1,0,2:T(8,128)}, u32[]{:S(2)}, u32[]{:S(2)}) %all-to-all-start) | async-done | bytes 5505056 | tf_op jit(solution)/shard_map/all_to_all | solution.py:11
  206.8 5.8 %fusion.7 = f32[3,7,16,256,1]{3,2,0,1,4:T(8,128)S(1)} fusion(f32[3,7,256,256,1]{3,1,0,2,4:T(8,128)} %bitcast.68, f32[3,7,16,7,256]{4,2,1,0,3:T(8,128)S(1)} %fusion.32), kind=kOutput, calls=%fused_computation.8 | convolution fusion | flops 924844032 | bytes 8257536 | tf_op jit(solution)/shard_map/ibcas,iasr->ibcr/dot_general | solution.py:70
  212.6 0.1 bitcast_multiply_fusion.1
  212.8 6.1 %collective-permute-start.6 = (f32[15,16,256]{2,1,0:T(8,128)S(1)}, f32[15,16,256]{2,1,0:T(8,128)S(1)}, u32[]{:S(2)}, u32[]{:S(2)}) collective-permute-start(f32[15,16,256]{2,1,0:T(8,128)S(1)} %pad_maximum_fusion.6), channel_id=1, source_target_pairs={{0,16},{16,32},{32,48},{48,64},{64,80},{80,96},{96,112},{112,128},... | collective-permute-start | bytes 737288 | tf_op jit(solution)/shard_map/ppermute | solution.py:16
  219.0 0.0 collective-permute-start.7
  219.0 3.1 %collective-permute-done.6 = f32[15,16,256]{2,1,0:T(8,128)S(1)} collective-permute-done((f32[15,16,256]{2,1,0:T(8,128)S(1)}, f32[15,16,256]{2,1,0:T(8,128)S(1)}, u32[]{:S(2)}, u32[]{:S(2)}) %collective-permute-start.6) | collective-permute-done | bytes 245792 | tf_op jit(solution)/shard_map/ppermute | solution.py:16
  222.3 0.1 bitcast_dynamic-update-slice_fusion.1
  222.4 2.2 collective-permute-done.7
  224.7 0.1 fusion.81
  224.9 6.1 %fusion.5 = f32[3,7,16,256,1]{3,2,0,1,4:T(8,128)S(1)} fusion(f32[3,7,256,256,1]{3,1,0,2,4:T(8,128)} %bitcast.68, f32[3,7,16,7,256]{4,2,1,0,3:T(8,128)S(1)} %fusion.20), kind=kOutput, calls=%fused_computation.6 | convolution fusion | flops 924844032 | bytes 8257536 | tf_op jit(solution)/shard_map/ibcas,iasr->ibcr/dot_general | solution.py:70
  230.9 0.9 fusion.78
  (101 shorter events, 1.6 us)
Async XLA Ops:
  6.5 82.2 %all-gather.2.cloned.1.call-start = ((), (), s32[]{:S(2)}) async-start(), calls=%async_computation.1 | async-start | bytes 5849088 | tf_op jit(solution)/shard_map/all_gather | solution.py:79
  9.1 8.9 %copy-start.1 = (pred[7]{0:T(512)(128)(4,1)S(1)}, pred[7]{0:T(512)(128)(4,1)}, u32[]{:S(2)}) copy-start(pred[7]{0:T(512)(128)(4,1)} %constant.7.clone.1) | copy-start | bytes 25
  9.2 7.9 %collective-permute-start = (f32[15,16,256]{2,1,0:T(8,128)S(1)}, f32[15,16,256]{2,1,0:T(8,128)S(1)}, u32[]{:S(2)}, u32[]{:S(2)}) collective-permute-start(f32[15,16,256]{2,1,0:T(8,128)S(1)} %pad_maximum_fusion), channel_id=1, source_target_pairs={{0,16},{16,32},{32,48},{48,64},{64,80},{80,96},{96,112},{112,128},... | collective-permute-start | bytes 737288 | tf_op jit(solution)/shard_map/ppermute | solution.py:16
  12.2 5.9 %copy-start = (f32[3,7,16,256]{3,2,1,0:T(8,128)S(1)}, f32[3,7,16,256]{3,2,1,0:T(8,128)}, u32[]{:S(2)}) copy-start(f32[3,7,16,256]{3,2,1,0:T(8,128)} %param.2) | copy-start | bytes 1032196
  12.2 5.6 %collective-permute-start.1 = (f32[15,16,256]{2,1,0:T(8,128)S(1)}, f32[15,16,256]{2,1,0:T(8,128)S(1)}, u32[]{:S(2)}, u32[]{:S(2)}) collective-permute-start(f32[15,16,256]{2,1,0:T(8,128)S(1)} %pad_maximum_fusion.1), channel_id=1, source_target_pairs={{0,496},{16,0},{32,16},{48,32},{64,48},{80,64},{96,80},{112,96},{1... | collective-permute-start | bytes 737288 | tf_op jit(solution)/shard_map/ppermute | solution.py:16
  88.7 12.4 %slice-start = ((s8[5505024]{0:T(1024)(128)(4,1)}), s8[4194304]{0:T(1024)(128)(4,1)S(1)}, s32[]{:S(2)}) async-start(s8[5505024]{0:T(1024)(128)(4,1)} %bitcast.251), calls=%async_computation.2 | async-start | bytes 8388608
  93.1 8.0 %slice-start.1 = ((s8[5505024]{0:T(1024)(128)(4,1)}), s8[1310720]{0:T(1024)(128)(4,1)S(1)}, s32[]{:S(2)}) async-start(s8[5505024]{0:T(1024)(128)(4,1)} %bitcast.251), calls=%async_computation.3 | async-start | bytes 2621440
  93.2 5.0 %collective-permute-start.2 = (f32[15,16,256]{2,1,0:T(8,128)S(1)}, f32[15,16,256]{2,1,0:T(8,128)S(1)}, u32[]{:S(2)}, u32[]{:S(2)}) collective-permute-start(f32[15,16,256]{2,1,0:T(8,128)S(1)} %pad_maximum_fusion.2), channel_id=1, source_target_pairs={{0,16},{16,32},{32,48},{48,64},{64,80},{80,96},{96,112},{112,128},... | collective-permute-start | bytes 737288 | tf_op jit(solution)/shard_map/ppermute | solution.py:16
  95.1 5.8 %collective-permute-start.3 = (f32[15,16,256]{2,1,0:T(8,128)S(1)}, f32[15,16,256]{2,1,0:T(8,128)S(1)}, u32[]{:S(2)}, u32[]{:S(2)}) collective-permute-start(f32[15,16,256]{2,1,0:T(8,128)S(1)} %pad_maximum_fusion.3), channel_id=1, source_target_pairs={{0,496},{16,0},{32,16},{48,32},{64,48},{80,64},{96,80},{112,96},{1... | collective-permute-start | bytes 737288 | tf_op jit(solution)/shard_map/ppermute | solution.py:16
  109.3 97.5 %all-to-all-start = ((f32[3,7,256,256]{3,1,0,2:T(8,128)}), f32[3,7,256,256]{3,1,0,2:T(8,128)}, u32[]{:S(2)}, u32[]{:S(2)}) async-start(f32[3,7,256,256]{3,1,0,2:T(8,128)} %copy.19), calls=%async_computation | async-start | bytes 12582912 | tf_op jit(solution)/shard_map/all_to_all | solution.py:11
  114.5 3.5 %collective-permute-start.4 = (f32[15,16,256]{2,1,0:T(8,128)S(1)}, f32[15,16,256]{2,1,0:T(8,128)S(1)}, u32[]{:S(2)}, u32[]{:S(2)}) collective-permute-start(f32[15,16,256]{2,1,0:T(8,128)S(1)} %pad_maximum_fusion.4), channel_id=1, source_target_pairs={{0,16},{16,32},{32,48},{48,64},{64,80},{80,96},{96,112},{112,128},... | collective-permute-start | bytes 737288 | tf_op jit(solution)/shard_map/ppermute | solution.py:16
  114.8 6.0 %collective-permute-start.5 = (f32[15,16,256]{2,1,0:T(8,128)S(1)}, f32[15,16,256]{2,1,0:T(8,128)S(1)}, u32[]{:S(2)}, u32[]{:S(2)}) collective-permute-start(f32[15,16,256]{2,1,0:T(8,128)S(1)} %pad_maximum_fusion.5), channel_id=1, source_target_pairs={{0,496},{16,0},{32,16},{48,32},{64,48},{80,64},{96,80},{112,96},{1... | collective-permute-start | bytes 737288 | tf_op jit(solution)/shard_map/ppermute | solution.py:16
  212.8 9.3 %collective-permute-start.6 = (f32[15,16,256]{2,1,0:T(8,128)S(1)}, f32[15,16,256]{2,1,0:T(8,128)S(1)}, u32[]{:S(2)}, u32[]{:S(2)}) collective-permute-start(f32[15,16,256]{2,1,0:T(8,128)S(1)} %pad_maximum_fusion.6), channel_id=1, source_target_pairs={{0,16},{16,32},{32,48},{48,64},{64,80},{80,96},{96,112},{112,128},... | collective-permute-start | bytes 737288 | tf_op jit(solution)/shard_map/ppermute | solution.py:16
  219.0 5.6 %collective-permute-start.7 = (f32[15,16,256]{2,1,0:T(8,128)S(1)}, f32[15,16,256]{2,1,0:T(8,128)S(1)}, u32[]{:S(2)}, u32[]{:S(2)}) collective-permute-start(f32[15,16,256]{2,1,0:T(8,128)S(1)} %pad_maximum_fusion.7), channel_id=1, source_target_pairs={{0,496},{16,0},{32,16},{48,32},{64,48},{80,64},{96,80},{112,96},{1... | collective-permute-start | bytes 737288 | tf_op jit(solution)/shard_map/ppermute | solution.py:16
Sparse Core Ops, SparseCore 0:
  10.4 78.2 all-gather.1
